TPU v7x, 512 devices: a whole 4x4x16 slice. The times are simulated.
512 devices in a mesh: gx: 8 (over x, core), gy: 4 (over y), gz: 16 (over z).
Axes of the slice: x: 4, y: 4, z: 16, core: 2. Of those that a mesh axis runs over, the one named last changes fastest.
Arguments:
- multipoles: bfloat16 [289, 262144], P(None, ('gx', 'gy', 'gz')), may hold values from -6 to 6
- up_shift: bfloat16 [8, 289, 289], replicated, may hold values from -0.125 to 0.125
- down_shift: bfloat16 [8, 289, 289], replicated, may hold values from -0.375 to 0.375
- far_shift: bfloat16 [8, 289, 289], replicated, may hold values from -0.09375 to 0.09375
- send_list: int32 [8, 64, 64, 16], P('gx', ('gy', 'gz')), may hold values from 0 to 511
- leaf_src: int32 [16, 262144], P(None, ('gx', 'gy', 'gz')), may hold values from 0 to 1535
- leaf_kind: int32 [16, 262144], P(None, ('gx', 'gy', 'gz')), may hold values from 0 to 7
- coarse_src: int32 [8, 64], replicated, may hold values from 0 to 63
- coarse_kind: int32 [8, 64], replicated, may hold values from 0 to 7
Outputs:
- leaf_local: bfloat16 [289, 262144], P(None, ('gx', 'gy', 'gz'))
All inputs are finite; a program needn't handle non-finite values.
Results may differ from a plain program's by a relative error of at most 0.014.
Values may be sent and summed in bfloat16 or wider, within the bound.
No kernel may reach another device: no remote copies, remote signals or barrier semaphores. Data moves between devices by JAX's collectives and lax.ppermute only.
A program may use at most 128 MiB of HBM per device.

v0:
```python
import jax
import jax.numpy as jnp
from jax import lax
from jax.sharding import PartitionSpec as P

LOCAL_LEVELS = 3


def lift_level(children, up_shift):
    coefs = children.shape[0]
    count = children.shape[1] // 8
    child_stack = children.reshape(coefs, count, 8).transpose(2, 0, 1).reshape(8 * coefs, count)
    shift_table = up_shift.transpose(1, 0, 2).reshape(coefs, 8 * coefs)
    return jnp.dot(shift_table, child_stack, preferred_element_type=jnp.float32)


def lower_level(parent, down_shift):
    coefs = parent.shape[0]
    count = parent.shape[1]
    spread = jnp.dot(
        down_shift.reshape(8 * coefs, coefs), parent, preferred_element_type=jnp.float32
    )
    return spread.reshape(8, coefs, count).transpose(1, 2, 0).reshape(coefs, 8 * count)


def on_device(
    multipoles,
    up_shift,
    down_shift,
    far_shift,
    send_list,
    leaf_src,
    leaf_kind,
    coarse_src,
    coarse_kind,
):
    coefs = multipoles.shape[0]
    kind_count = far_shift.shape[0]
    flat_index = lax.axis_index(("gx", "gy", "gz"))
    coarse_box = flat_index // 8
    octant = flat_index % 8
    peer_count = lax.axis_size(("gy", "gz"))
    slot_count = send_list.shape[3]
    send_order = send_list.reshape(peer_count * slot_count)
    outgoing = jnp.take(multipoles, send_order, axis=1)
    arrived = lax.all_to_all(outgoing, ("gy", "gz"), split_axis=1, concat_axis=1, tiled=True)
    upward = multipoles
    for level in range(LOCAL_LEVELS):
        upward = lift_level(upward, up_shift).astype(jnp.bfloat16)
    every_box = lax.all_gather(upward, ("gx", "gy", "gz"), axis=1, tiled=True)
    coarse_multi = lift_level(every_box, up_shift).astype(jnp.bfloat16)
    coarse_cols = coarse_src[:, coarse_box]
    coarse_kinds = coarse_kind[:, coarse_box]
    list_len = coarse_cols.shape[0]
    coarse_picked = jnp.take(coarse_multi, coarse_cols, axis=1)
    stacked = (
        jnp.take(far_shift, coarse_kinds, axis=0)
        .transpose(1, 0, 2)
        .reshape(coefs, list_len * coefs)
    )
    column_vec = coarse_picked.transpose(1, 0).reshape(list_len * coefs, 1)
    coarse_local = jnp.dot(stacked, column_vec, preferred_element_type=jnp.float32).astype(
        jnp.bfloat16
    )
    downward = jnp.dot(down_shift[octant], coarse_local, preferred_element_type=jnp.float32).astype(
        jnp.bfloat16
    )
    for level in range(LOCAL_LEVELS - 1):
        downward = lower_level(downward, down_shift).astype(jnp.bfloat16)
    chain_part = lower_level(downward, down_shift)
    buffer = jnp.concatenate([multipoles, arrived], axis=1)
    leaf_count = leaf_src.shape[1]
    picked = jnp.take(buffer, leaf_src, axis=1)
    kind_range = jnp.arange(kind_count, dtype=jnp.int32)
    kind_hot = (leaf_kind[None, :, :] == kind_range[:, None, None]).astype(jnp.bfloat16)
    grouped = jnp.einsum("plt,klt->kpt", picked, kind_hot, preferred_element_type=jnp.float32)
    grouped = grouped.reshape(kind_count * coefs, leaf_count)
    upper_part = grouped.astype(jnp.bfloat16)
    lower_part = (grouped - upper_part.astype(jnp.float32)).astype(jnp.bfloat16)
    shift_table = far_shift.transpose(1, 0, 2).reshape(coefs, kind_count * coefs)
    far_total = jnp.dot(shift_table, upper_part, preferred_element_type=jnp.float32)
    far_total = far_total + jnp.dot(shift_table, lower_part, preferred_element_type=jnp.float32)
    return (chain_part + far_total).astype(jnp.bfloat16)


def solution(mesh):
    in_specs = (
        P(None, ("gx", "gy", "gz")),
        P(),
        P(),
        P(),
        P("gx", ("gy", "gz"), None, None),
        P(None, ("gx", "gy", "gz")),
        P(None, ("gx", "gy", "gz")),
        P(),
        P(),
    )
    out_specs = P(None, ("gx", "gy", "gz"))
    return jax.shard_map(
        on_device, mesh=mesh, in_specs=in_specs, out_specs=out_specs, check_vma=False
    )
```

profile of v0, /device:TPU:32, one launch (start us, length us, event | category | flops | bytes accessed | tf_op | source)
XLA Modules:
  0.0 275.0 jit_solution(4691575993083344755)
XLA Ops:
  0.0 0.8 copy.104
  0.8 0.7 compare_and_fusion.1
  1.5 1.2 copy.91
  2.7 0.1 reshape.143
  2.8 0.1 copy.103
  2.9 3.9 %gather_fusion.2 = bf16[1024,289]{1,0:T(8,128)(2,1)S(1)} fusion(bf16[289,512]{0,1:T(8,128)(2,1)S(1)} %copy.91, s32[1024]{0:T(1024)S(1)} %broadcast_clamp_fusion.1), kind=kCustom, calls=%fused_computation.2 | custom fusion | bytes 1187840 | tf_op jit(solution)/shard_map/jit(_take)/gather | solution.py:45
  6.8 0.0 copy-start.9
  6.8 0.0 copy-start.10
  6.8 1.1 broadcast_select_fusion
  7.9 18.4 %all-to-all-start = ((bf16[289,64,16]{0,2,1:T(8,128)(2,1)}), bf16[289,64,16]{0,2,1:T(8,128)(2,1)S(1)}, u32[]{:S(2)}, u32[]{:S(2)}) async-start(bf16[289,64,16]{0,2,1:T(8,128)(2,1)} %broadcast_select_fusion), calls=%async_computation | async-start | bytes 1572864 | tf_op jit(solution)/shard_map/all_to_all | solution.py:46
  26.3 0.2 fusion.74
  26.5 0.2 and_reduce_fusion
  26.8 0.2 fusion.75
  27.0 3.0 %reshape.137 = bf16[289,2312]{1,0:T(8,128)(2,1)} reshape(bf16[289,8,289]{2,1,0:T(8,128)(2,1)S(1)} %bitcast.160) | data formatting | bytes 2672672 | tf_op jit(solution)/shard_map/reshape | solution.py:13
  29.9 0.7 fusion.45
  30.7 0.6 fusion.57
  31.3 0.1 reshape.185
  31.4 2.0 convolution_reduce_fusion.1
  33.4 151.1 %all-gather = bf16[512,1,289]{2,1,0:T(2,128)(2,1)S(1)} all-gather(bf16[1,1,289]{2,1,0:T(2,128)(2,1)S(1)} %reshape.178), channel_id=1, replica_groups=mesh['gx'=8,'gy'=4,'gz'=16] {'gx','gy','gz'}, dimensions={0}, use_global_device_ids=true | all-gather | bytes 296514 | tf_op jit(solution)/shard_map/all_gather | solution.py:50
  184.5 0.1 copy.180
  184.6 0.7 fusion.48
  185.4 0.6 gather_fusion.1
  185.9 0.1 select_bitcast_fusion.1
  186.0 0.1 copy-done
  186.1 6.8 %gather_fusion = bf16[8,289,289]{2,0,1:T(8,128)(2,1)} fusion(bf16[8,289,289]{2,0,1:T(8,128)(2,1)S(1)} %copy-done, s32[1024]{0:T(1024)S(1)} %pad_clamp_fusion.1), kind=kCustom, calls=%fused_computation | custom fusion | bytes 2672704 | tf_op jit(solution)/shard_map/jit(_take)/gather | solution.py:57
  192.9 1.8 select_bitcast_fusion
  194.7 0.6 fusion.60
  195.3 4.5 %copy.100 = bf16[8,289,289]{1,0,2:T(8,128)(2,1)} copy(bf16[8,289,289]{2,0,1:T(8,128)(2,1)} %param.11) | data formatting | bytes 2672672 | tf_op args[2]
  199.8 1.9 constant_dynamic-slice_fusion
  201.7 0.2 convolution_reduce_fusion
  202.0 4.1 %reshape.139 = bf16[2312,289]{0,1:T(8,128)(2,1)} reshape(bf16[8,289,289]{1,0,2:T(8,128)(2,1)} %copy.100) | data formatting | bytes 2672672 | tf_op jit(solution)/shard_map/reshape | solution.py:21
  206.0 2.3 fusion.8
  208.3 0.3 fusion.4
  208.7 0.1 convert_element_type.88
  208.8 2.6 convolution_bitcast_fusion
  211.4 2.4 reshape.140
  213.8 2.2 copy.113
  216.0 0.1 copy.101
  216.2 0.2 copy.102
  216.4 3.2 %copy.119 = bf16[289,8,289]{0,1,2:T(8,128)(2,1)} copy(bf16[289,8,289]{2,1,0:T(8,128)(2,1)S(1)} %bitcast.158) | data formatting | bytes 2672672 | tf_op jit(solution)/shard_map/transpose | solution.py:80
  219.5 0.1 pad_maximum_fusion
  219.7 33.2 %gather_fusion.3 = bf16[8192,289]{1,0:T(8,128)(2,1)} fusion(bf16[289,1536]{0,1:T(8,128)(2,1)S(1)} %pad_maximum_fusion, s32[8192]{0:T(1024)S(1)} %broadcast_clamp_fusion), kind=kCustom, calls=%fused_computation.3 | custom fusion | bytes 9502720 | tf_op jit(solution)/shard_map/jit(_take)/gather | solution.py:73
  252.9 10.0 %fusion = f32[512,8,289]{2,1,0:T(8,128)} fusion(bf16[16,512,289]{2,1,0:T(8,128)(2,1)} %bitcast.164, pred[16,512]{0,1:T(8,128)(4,1)S(1)} %copy.102, s32[16,512]{0,1:T(8,128)S(1)} %copy.101), kind=kOutput, calls=%fused_computation.4 | convolution fusion | flops 40312832 | bytes 9510912 | tf_op jit(solution)/shard_map/plt,klt->kpt/dot_general | solution.py:76
  262.8 6.5 %copy.108 = f32[512,8,289]{0,1,2:T(8,128)} copy(f32[512,8,289]{2,1,0:T(8,128)} %fusion) | data formatting | bytes 9469952 | tf_op jit(solution)/shard_map/plt,klt->kpt/dot_general | solution.py:76
  269.3 3.5 %convolution_bitcast_fusion.1 = f32[512,289]{0,1:T(8,128)S(1)} fusion(bf16[289,8,289]{0,1,2:T(8,128)(2,1)S(1)} %copy-done.5, f32[512,8,289]{0,1,2:T(8,128)} %copy.108), kind=kOutput, calls=%fused_computation.29 | convolution fusion | flops 684204032 | bytes 6663184 | tf_op jit(solution)/shard_map/dot_general | solution.py:81
  272.9 0.2 copy-done.1
  273.1 0.2 copy-done.6
  273.2 1.7 fusion.30
  (29 shorter events, 0.1 us)
Async XLA Ops:
  6.8 19.5 %copy-start.9 = (s32[8,64]{1,0:T(8,128)S(1)}, s32[8,64]{1,0:T(8,128)}, u32[]{:S(2)}) copy-start(s32[8,64]{1,0:T(8,128)} %param.17) | copy-start | bytes 6148
  6.8 19.7 %copy-start.10 = (s32[8,64]{1,0:T(8,128)S(1)}, s32[8,64]{1,0:T(8,128)}, u32[]{:S(2)}) copy-start(s32[8,64]{1,0:T(8,128)} %param.16) | copy-start | bytes 6148
  6.8 20.2 %copy-start.3 = (bf16[8,289,289]{2,0,1:T(8,128)(2,1)S(1)}, bf16[8,289,289]{2,0,1:T(8,128)(2,1)}, u32[]{:S(2)}) copy-start(bf16[8,289,289]{2,0,1:T(8,128)(2,1)} %param.10) | copy-start | bytes 4009012
  7.9 211.6 %all-to-all-start = ((bf16[289,64,16]{0,2,1:T(8,128)(2,1)}), bf16[289,64,16]{0,2,1:T(8,128)(2,1)S(1)}, u32[]{:S(2)}, u32[]{:S(2)}) async-start(bf16[289,64,16]{0,2,1:T(8,128)(2,1)} %broadcast_select_fusion), calls=%async_computation | async-start | bytes 1572864 | tf_op jit(solution)/shard_map/all_to_all | solution.py:46
  31.4 153.2 %copy-start.4 = (bf16[8,289,289]{2,0,1:T(8,128)(2,1)S(1)}, bf16[8,289,289]{2,0,1:T(8,128)(2,1)}, u32[]{:S(2)}) copy-start(bf16[8,289,289]{2,0,1:T(8,128)(2,1)} %param.10) | copy-start | bytes 4009012
  184.6 1.5 copy-start
  206.0 2.3 copy-start.2
  211.4 4.6 %copy-start.7 = (s32[16,512]{1,0:T(8,128)S(1)}, s32[16,512]{1,0:T(8,128)}, u32[]{:S(2)}) copy-start(s32[16,512]{1,0:T(8,128)} %param.14) | copy-start | bytes 98308
  211.4 4.6 %copy-start.8 = (s32[16,512]{1,0:T(8,128)S(1)}, s32[16,512]{1,0:T(8,128)}, u32[]{:S(2)}) copy-start(s32[16,512]{1,0:T(8,128)} %param.15) | copy-start | bytes 98308
  262.8 6.5 %copy-start.5 = (bf16[289,8,289]{0,1,2:T(8,128)(2,1)S(1)}, bf16[289,8,289]{0,1,2:T(8,128)(2,1)}, u32[]{:S(2)}) copy-start(bf16[289,8,289]{0,1,2:T(8,128)(2,1)} %copy.119) | copy-start | bytes 4009012
  269.3 3.8 %copy-start.1 = (f32[512,8,289]{0,1,2:T(8,128)S(1)}, f32[512,8,289]{0,1,2:T(8,128)}, u32[]{:S(2)}) copy-start(f32[512,8,289]{0,1,2:T(8,128)} %copy.108) | copy-start | bytes 14204932
  269.3 3.9 %copy-start.6 = (f32[289,512]{1,0:T(8,128)S(1)}, f32[289,512]{1,0:T(8,128)}, u32[]{:S(2)}) copy-start(f32[289,512]{1,0:T(8,128)} %copy.113) | copy-start | bytes 1775620
where the time goes:
time: 276 us; the launch traced here: 275 us
  blocking collectives  151 us (55%)
  local copies, waits for them, and re-layouts  75.5 us (27%)
  matrix products  25.2 us (9%)
  starting transfers between devices  18.4 us (7%)
  other arithmetic  4.45 us (2%)
    all_gather x1, blocking collectives, on_device(): every_box = lax.all_gather(upward, ('gx', 'gy', 'gz'), axis=1, tiled=True)  151 us
    gather x1, local copies, waits for them, and re-layouts, on_device(): picked = jnp.take(buffer, leaf_src, axis=1)  33.2 us
    all_to_all x1, starting transfers between devices, on_device(): lax.all_to_all(outgoing, ('gy', 'gz'), split_axis=1, concat_axis=1, tiled...  18.4 us
    dot_general x1, matrix products, on_device(): jnp.einsum('plt,klt->kpt', picked, kind_hot, preferred_element_type=jnp.f...  9.96 us
    unnamed x29, local copies, waits for them, and re-layouts  7.11 us
    gather x1, local copies, waits for them, and re-layouts, on_device(): jnp.take(far_shift, coarse_kinds, axis=0).transpose(1, 0, 2)  6.81 us
    dot_general x1, local copies, waits for them, and re-layouts, on_device(): jnp.einsum('plt,klt->kpt', picked, kind_hot, preferred_element_type=jnp.f...  6.5 us
  transfers between devices with their start and end apart: 1, of which 0 were waited for; matrix products, arithmetic and copies ran while one was open for 15% of the time, Pallas kernels for 0%

commit v1 on v0

--- a/solution.py
+++ b/solution.py
@@ -2,6 +2,7 @@
 import jax.numpy as jnp
 from jax import lax
 from jax.sharding import PartitionSpec as P
+from jax.lax import all_to_all, psum
 
 LOCAL_LEVELS = 3
 
@@ -47,7 +48,10 @@
     upward = multipoles
     for level in range(LOCAL_LEVELS):
         upward = lift_level(upward, up_shift).astype(jnp.bfloat16)
-    every_box = lax.all_gather(upward, ("gx", "gy", "gz"), axis=1, tiled=True)
+    press_the_turns = lambda local_x, shard_axis: jnp.concatenate(
+        all_to_all(jnp.stack(psum(1, shard_axis) * [local_x], 0), shard_axis, 0, 0), 1
+    )
+    every_box = press_the_turns(upward, ("gx", "gy", "gz"))
     coarse_multi = lift_level(every_box, up_shift).astype(jnp.bfloat16)
     coarse_cols = coarse_src[:, coarse_box]
     coarse_kinds = coarse_kind[:, coarse_box]

time: 276 us -> 185 us (0.67)
  the two profiles are of different devices: /device:TPU:32 before, /device:TPU:10 now
where the time goes in v1:
time: 185 us; the launch traced here: 184 us
  local copies, waits for them, and re-layouts  73.8 us (40%)
  waiting for transfers between devices  50.4 us (27%)
  starting transfers between devices  29.6 us (16%)
  matrix products  22.9 us (12%)
  other arithmetic  7.35 us (4%)
    all_to_all x1, waiting for transfers between devices, on_device(): all_to_all(jnp.stack(psum(1, shard_axis) * [local_x], 0), shard_axis, 0, 0)  37 us
    gather x1, local copies, waits for them, and re-layouts, on_device(): picked = jnp.take(buffer, leaf_src, axis=1)  33.2 us
    all_to_all x1, starting transfers between devices, on_device(): all_to_all(jnp.stack(psum(1, shard_axis) * [local_x], 0), shard_axis, 0, 0)  23.2 us
    all_to_all x1, waiting for transfers between devices, on_device(): lax.all_to_all(outgoing, ('gy', 'gz'), split_axis=1, concat_axis=1, tiled...  13.4 us
    dot_general x1, matrix products, on_device(): jnp.einsum('plt,klt->kpt', picked, kind_hot, preferred_element_type=jnp.f...  9.96 us
    gather x1, local copies, waits for them, and re-layouts, on_device(): jnp.take(far_shift, coarse_kinds, axis=0).transpose(1, 0, 2)  6.81 us
    dot_general x1, local copies, waits for them, and re-layouts, on_device(): jnp.einsum('plt,klt->kpt', picked, kind_hot, preferred_element_type=jnp.f...  6.5 us
    all_to_all x1, starting transfers between devices, on_device(): lax.all_to_all(outgoing, ('gy', 'gz'), split_axis=1, concat_axis=1, tiled...  6.35 us
  transfers between devices with their start and end apart: 2, of which 2 were waited for; matrix products, arithmetic and copies ran while one was open for 20% of the time, Pallas kernels for 0%

profile of v1, /device:TPU:10, one launch (start us, length us, event | category | flops | bytes accessed | tf_op | source)
XLA Modules:
  0.0 184.4 jit_solution(4358910705173916672)
XLA Ops:
  0.0 1.2 copy.67
  1.2 4.2 %reshape.140 = bf16[289,2312]{1,0:T(8,128)(2,1)} reshape(bf16[289,8,289]{2,1,0:T(8,128)(2,1)} %bitcast.158) | data formatting | bytes 2672672 | tf_op jit(solution)/shard_map/reshape | solution.py:14
  5.4 0.7 fusion.45
  6.1 0.6 fusion.57
  6.7 0.1 reshape.183
  6.9 0.0 copy-start.11
  6.9 1.9 %convolution_reduce_fusion.1 = bf16[289]{0:T(512)(128)(2,1)S(1)} fusion(bf16[2312,1]{0,1:T(2,128)(2,1)S(1)} %reshape.183, bf16[289,2312]{1,0:T(8,128)(2,1)} %reshape.140), kind=kOutput, calls=%fused_computation.46 | convolution fusion | flops 1336336 | bytes 1341538 | tf_op jit(solution)/shard_map/dot_general | solution.py:15
  8.7 1.3 stack.2
  10.0 23.2 %all-to-all-start = ((bf16[512,289,1]{1,2,0:T(2,128)(2,1)}), bf16[512,289,1]{1,2,0:T(2,128)(2,1)S(1)}, u32[]{:S(2)}, u32[]{:S(2)}) async-start(bf16[512,289,1]{1,2,0:T(2,128)(2,1)} %stack.2), calls=%async_computation | async-start | bytes 1572864 | tf_op jit(solution)/shard_map/all_to_all | solution.py:52
  33.3 0.1 copy.79
  33.4 0.1 reshape.146
  33.5 0.0 copy-start.12
  33.5 5.0 %gather_fusion.2 = bf16[1024,289]{1,0:T(8,128)(2,1)} fusion(bf16[289,512]{0,1:T(8,128)(2,1)S(1)} %copy.67, s32[1024]{0:T(1024)S(1)} %broadcast_clamp_fusion.1), kind=kCustom, calls=%fused_computation.2 | custom fusion | bytes 1187840 | tf_op jit(solution)/shard_map/jit(_take)/gather | solution.py:46
  38.5 0.1 copy.78
  38.6 0.2 fusion.74
  38.8 0.2 fusion.75
  39.1 2.2 %broadcast_select_fusion = bf16[289,64,16]{0,2,1:T(8,128)(2,1)} fusion(bf16[289,64,16]{0,2,1:T(8,128)(2,1)} %bitcast.164, pred[64,16]{1,0:T(8,128)(4,1)S(1)} %copy.78), kind=kLoop, calls=%fused_computation.48 | loop fusion | flops 295936 | bytes 1184768 | tf_op jit(solution)/shard_map/jit(_take)/select_n | solution.py:46
  41.3 37.0 %all-to-all-done = bf16[512,289,1]{1,2,0:T(2,128)(2,1)S(1)} async-done(((bf16[512,289,1]{1,2,0:T(2,128)(2,1)}), bf16[512,289,1]{1,2,0:T(2,128)(2,1)S(1)}, u32[]{:S(2)}, u32[]{:S(2)}) %all-to-all-start) | async-done | bytes 295968 | tf_op jit(solution)/shard_map/all_to_all | solution.py:52
  78.3 6.3 %all-to-all-start.1 = ((bf16[289,64,16]{0,2,1:T(8,128)(2,1)}), bf16[289,64,16]{0,2,1:T(8,128)(2,1)}, u32[]{:S(2)}, u32[]{:S(2)}) async-start(bf16[289,64,16]{0,2,1:T(8,128)(2,1)} %broadcast_select_fusion), calls=%async_computation.1 | async-start | bytes 1572864 | tf_op jit(solution)/shard_map/all_to_all | solution.py:47
  84.7 3.1 %copy.75 = bf16[8,289,289]{1,0,2:T(8,128)(2,1)} copy(bf16[8,289,289]{2,0,1:T(8,128)(2,1)S(1)} %copy-done.3) | data formatting | bytes 2672672 | tf_op args[2]
  87.9 4.2 %reshape.142 = bf16[2312,289]{0,1:T(8,128)(2,1)} reshape(bf16[8,289,289]{1,0,2:T(8,128)(2,1)} %copy.75) | data formatting | bytes 2672672 | tf_op jit(solution)/shard_map/reshape | solution.py:22
  92.1 0.8 copy.76
  92.9 0.2 copy.77
  93.1 6.8 %gather_fusion = bf16[8,289,289]{2,0,1:T(8,128)(2,1)} fusion(bf16[8,289,289]{2,0,1:T(8,128)(2,1)S(1)} %copy-done, s32[1024]{0:T(1024)S(1)} %pad_clamp_fusion.1), kind=kCustom, calls=%fused_computation | custom fusion | bytes 2672704 | tf_op jit(solution)/shard_map/jit(_take)/gather | solution.py:61
  99.9 3.2 %copy.94 = bf16[289,8,289]{0,1,2:T(8,128)(2,1)} copy(bf16[289,8,289]{2,1,0:T(8,128)(2,1)S(1)} %bitcast.156) | data formatting | bytes 2672672 | tf_op jit(solution)/shard_map/transpose | solution.py:84
  103.1 0.2 and_reduce_fusion
  103.3 1.9 %constant_dynamic-slice_fusion = bf16[1,289,289]{2,0,1:T(2,128)(2,1)S(1)} fusion(bf16[8,289,289]{2,0,1:T(8,128)(2,1)} %param.11, s32[]{:T(128)S(6)} %select_n.79), kind=kLoop, calls=%fused_computation.77 | loop fusion | bytes 334088 | tf_op jit(solution)/shard_map/dynamic_slice | solution.py:69
  105.3 3.1 %select_bitcast_fusion = bf16[289,8,289]{2,1,0:T(8,128)(2,1)} fusion(bf16[8,289,289]{2,0,1:T(8,128)(2,1)} %gather_fusion, pred[8]{0:T(512)(128)(4,1)S(1)} %get-tuple-element.6), kind=kLoop, calls=%fused_computation.21 | loop fusion | flops 668168 | bytes 2672680 | tf_op jit(solution)/shard_map/jit(_take)/select_n | solution.py:61
  108.4 0.1 copy.154
  108.5 0.7 fusion.48
  109.2 0.6 gather_fusion.1
  109.8 0.1 select_bitcast_fusion.1
  109.9 2.2 %fusion.60 = bf16[289]{0:T(512)(128)(2,1)S(1)} fusion(bf16[289,8,289]{2,1,0:T(8,128)(2,1)} %select_bitcast_fusion, bf16[8,289,1]{1,0,2:T(8,128)(2,1)S(1)} %select_bitcast_fusion.1), kind=kOutput, calls=%fused_computation.44 | convolution fusion | flops 1336336 | bytes 1341538 | tf_op jit(solution)/shard_map/dot_general | solution.py:66
  112.2 0.2 convolution_reduce_fusion
  112.4 0.7 fusion.8
  113.1 0.3 fusion.4
  113.4 0.1 convert_element_type.85
  113.6 0.4 convolution_bitcast_fusion
  113.9 0.4 reshape.143
  114.4 0.2 copy.88
  114.6 13.4 %all-to-all-done.1 = bf16[289,64,16]{0,2,1:T(8,128)(2,1)} async-done(((bf16[289,64,16]{0,2,1:T(8,128)(2,1)}), bf16[289,64,16]{0,2,1:T(8,128)(2,1)}, u32[]{:S(2)}, u32[]{:S(2)}) %all-to-all-start.1) | async-done | bytes 591904 | tf_op jit(solution)/shard_map/all_to_all | solution.py:47
  128.0 1.3 pad_maximum_fusion
  129.3 33.2 %gather_fusion.3 = bf16[8192,289]{1,0:T(8,128)(2,1)} fusion(bf16[289,1536]{0,1:T(8,128)(2,1)S(1)} %pad_maximum_fusion, s32[8192]{0:T(1024)S(1)} %broadcast_clamp_fusion), kind=kCustom, calls=%fused_computation.3 | custom fusion | bytes 9502720 | tf_op jit(solution)/shard_map/jit(_take)/gather | solution.py:77
  162.5 10.0 %fusion = f32[512,8,289]{2,1,0:T(8,128)} fusion(bf16[16,512,289]{2,1,0:T(8,128)(2,1)} %bitcast.162, pred[16,512]{0,1:T(8,128)(4,1)S(1)} %copy.77, s32[16,512]{0,1:T(8,128)S(1)} %copy-done.8), kind=kOutput, calls=%fused_computation.4 | convolution fusion | flops 40312832 | bytes 9510912 | tf_op jit(solution)/shard_map/plt,klt->kpt/dot_general | solution.py:80
  172.5 6.5 %copy.83 = f32[512,8,289]{0,1,2:T(8,128)} copy(f32[512,8,289]{2,1,0:T(8,128)} %fusion) | data formatting | bytes 9469952 | tf_op jit(solution)/shard_map/plt,klt->kpt/dot_general | solution.py:80
  179.0 3.5 %convolution_bitcast_fusion.1 = f32[512,289]{0,1:T(8,128)S(1)} fusion(bf16[289,8,289]{0,1,2:T(8,128)(2,1)S(1)} %copy-done.7, f32[512,8,289]{0,1,2:T(8,128)} %copy.83), kind=kOutput, calls=%fused_computation.29 | convolution fusion | flops 684204032 | bytes 6663184 | tf_op jit(solution)/shard_map/dot_general | solution.py:85
  182.5 0.2 copy-done.1
  182.7 1.7 fusion.30
  (36 shorter events, 0.1 us)
Async XLA Ops:
  1.2 4.2 %copy-start.5 = (bf16[8,289,289]{2,0,1:T(8,128)(2,1)S(1)}, bf16[8,289,289]{2,0,1:T(8,128)(2,1)}, u32[]{:S(2)}) copy-start(bf16[8,289,289]{2,0,1:T(8,128)(2,1)} %param.10) | copy-start | bytes 4009012
  6.9 26.4 %copy-start.11 = (s32[1,1,64,16]{2,3,1,0:T(8,128)S(1)}, s32[1,1,64,16]{2,3,1,0:T(8,128)}, u32[]{:S(2)}) copy-start(s32[1,1,64,16]{2,3,1,0:T(8,128)} %param.13) | copy-start | bytes 12292
  10.0 68.3 %all-to-all-start = ((bf16[512,289,1]{1,2,0:T(2,128)(2,1)}), bf16[512,289,1]{1,2,0:T(2,128)(2,1)S(1)}, u32[]{:S(2)}, u32[]{:S(2)}) async-start(bf16[512,289,1]{1,2,0:T(2,128)(2,1)} %stack.2), calls=%async_computation | async-start | bytes 1572864 | tf_op jit(solution)/shard_map/all_to_all | solution.py:52
  33.5 5.1 %copy-start.12 = (s32[8,64]{1,0:T(8,128)S(1)}, s32[8,64]{1,0:T(8,128)}, u32[]{:S(2)}) copy-start(s32[8,64]{1,0:T(8,128)} %param.17) | copy-start | bytes 6148
  33.5 5.3 %copy-start.13 = (s32[8,64]{1,0:T(8,128)S(1)}, s32[8,64]{1,0:T(8,128)}, u32[]{:S(2)}) copy-start(s32[8,64]{1,0:T(8,128)} %param.16) | copy-start | bytes 6148
  33.5 5.5 %copy-start.9 = (s32[16,512]{1,0:T(8,128)S(1)}, s32[16,512]{1,0:T(8,128)}, u32[]{:S(2)}) copy-start(s32[16,512]{1,0:T(8,128)} %param.14) | copy-start | bytes 98308
  38.5 46.2 %copy-start.3 = (bf16[8,289,289]{2,0,1:T(8,128)(2,1)S(1)}, bf16[8,289,289]{2,0,1:T(8,128)(2,1)}, u32[]{:S(2)}) copy-start(bf16[8,289,289]{2,0,1:T(8,128)(2,1)} %param.11) | copy-start | bytes 4009012
  78.3 49.7 %all-to-all-start.1 = ((bf16[289,64,16]{0,2,1:T(8,128)(2,1)}), bf16[289,64,16]{0,2,1:T(8,128)(2,1)}, u32[]{:S(2)}, u32[]{:S(2)}) async-start(bf16[289,64,16]{0,2,1:T(8,128)(2,1)} %broadcast_select_fusion), calls=%async_computation.1 | async-start | bytes 1572864 | tf_op jit(solution)/shard_map/all_to_all | solution.py:47
  87.9 4.2 %copy-start.10 = (s32[16,512]{1,0:T(8,128)S(1)}, s32[16,512]{1,0:T(8,128)}, u32[]{:S(2)}) copy-start(s32[16,512]{1,0:T(8,128)} %param.15) | copy-start | bytes 98308
  87.9 5.2 %copy-start = (bf16[8,289,289]{2,0,1:T(8,128)(2,1)S(1)}, bf16[8,289,289]{2,0,1:T(8,128)(2,1)}, u32[]{:S(2)}) copy-start(bf16[8,289,289]{2,0,1:T(8,128)(2,1)} %param.12) | copy-start | bytes 4009012
  105.3 3.2 %copy-start.6 = (bf16[8,289,289]{2,0,1:T(8,128)(2,1)S(1)}, bf16[8,289,289]{2,0,1:T(8,128)(2,1)}, u32[]{:S(2)}) copy-start(bf16[8,289,289]{2,0,1:T(8,128)(2,1)} %param.10) | copy-start | bytes 4009012
  109.8 2.6 %copy-start.4 = (bf16[8,289,289]{2,0,1:T(8,128)(2,1)S(1)}, bf16[8,289,289]{2,0,1:T(8,128)(2,1)}, u32[]{:S(2)}) copy-start(bf16[8,289,289]{2,0,1:T(8,128)(2,1)} %param.11) | copy-start | bytes 4009012
  109.9 3.2 %copy-start.2 = (bf16[2312,289]{0,1:T(8,128)(2,1)S(1)}, bf16[2312,289]{0,1:T(8,128)(2,1)}, u32[]{:S(2)}) copy-start(bf16[2312,289]{0,1:T(8,128)(2,1)} %reshape.142) | copy-start | bytes 4009012
  129.3 33.2 %copy-start.8 = (s32[16,512]{0,1:T(8,128)S(1)}, s32[16,512]{0,1:T(8,128)}, u32[]{:S(2)}) copy-start(s32[16,512]{0,1:T(8,128)} %copy.76) | copy-start | bytes 98308
  172.5 6.5 %copy-start.7 = (bf16[289,8,289]{0,1,2:T(8,128)(2,1)S(1)}, bf16[289,8,289]{0,1,2:T(8,128)(2,1)}, u32[]{:S(2)}) copy-start(bf16[289,8,289]{0,1,2:T(8,128)(2,1)} %copy.94) | copy-start | bytes 4009012
  179.0 3.8 %copy-start.1 = (f32[512,8,289]{0,1,2:T(8,128)S(1)}, f32[512,8,289]{0,1,2:T(8,128)}, u32[]{:S(2)}) copy-start(f32[512,8,289]{0,1,2:T(8,128)} %copy.83) | copy-start | bytes 14204932
